TPU v7x, 32 devices: a whole 2x2x4 slice. The times are simulated.
32 devices in a mesh: group: 2 (over y), ctx: 8 (over z, x), head: 2 (over core).
Axes of the slice: x: 2, y: 2, z: 4, core: 2. Of those that a mesh axis runs over, the one named last changes fastest.
Arguments:
- queries: bfloat16 [4096, 4096], P(('group', 'ctx'), 'head'), parts along dimension 0, may hold values from -7 to 7
- keys: bfloat16 [4096, 1024], P(('group', 'ctx'), 'head'), parts along dimension 0, may hold values from -4 to 4
- values: bfloat16 [4096, 1024], P(('group', 'ctx'), 'head'), parts along dimension 0, may hold values from -24 to 24
- doc_of_block: int32 [32], P('group'), parts along dimension 0, may hold values from 0 to 4, never falling along the last dimension, each value on 1 to 8 neighbouring positions
- out_weight: bfloat16 [4096, 4096], P('ctx', 'head'), may hold values from -0.09375 to 0.09375
Outputs:
- mixed: bfloat16 [4096, 4096], P(('group', 'ctx'), 'head'), parts along dimension 0
There are 2 independent parts, one for each index of `group`. A program takes and returns all parts, laid end to end along the dimension named above; an argument that names none is the same for every part. Nothing has to cross between parts.
Inputs may be any that keep to these rules, and one draw needn't show every extreme that they name: `doc_of_block`: blocks of one document are consecutive, and a document covers at most 8 blocks.
All inputs are finite; a program needn't handle non-finite values.
Results may differ from a plain program's by a relative error of at most 0.006.
Values may be sent and summed in bfloat16 or wider, within the bound.
No kernel may reach another device: no remote copies, remote signals or barrier semaphores. Data moves between devices by JAX's collectives and lax.ppermute only.
A program may use at most 64 MiB of HBM per device.

v0:
```python
import math
import jax
import jax.numpy as jnp
from jax import lax
from jax.sharding import PartitionSpec as P

HEAD_SIZE = 128
BLOCK_TOKENS = 128


def passed_along(array, axis, by):
    peers = lax.axis_size(axis)
    pairs = [(i, i + by) for i in range(peers) if 0 <= i + by < peers]
    return lax.ppermute(array, axis, pairs)


def lookup_docs(positions, doc_of_block):
    block_ids = jnp.floor_divide(positions, BLOCK_TOKENS)
    table_ids = jnp.arange(doc_of_block.shape[0], dtype=jnp.int32)
    matches = block_ids[:, None] == table_ids[None, :]
    return jnp.max(jnp.where(matches, doc_of_block[None, :], -1), axis=1)


def update(state_now, query_head_rows, key_piece, value_piece, visible):
    running_max, summed, totals = state_now
    rows_here = key_piece.shape[0]
    kv_heads = query_head_rows.shape[1]
    key_head_rows = key_piece.reshape(rows_here, kv_heads, HEAD_SIZE)
    value_head_rows = value_piece.reshape(rows_here, kv_heads, HEAD_SIZE)
    score_scale = 1.0 / math.sqrt(HEAD_SIZE)
    scores = (
        jnp.einsum(
            "qhgd,khd->hgqk", query_head_rows, key_head_rows, preferred_element_type=jnp.float32
        )
        * score_scale
    )
    scores = jnp.where(visible, scores, -1e30)
    new_max = jnp.maximum(running_max, jnp.max(scores, axis=-1))
    weights = jnp.where(visible, jnp.exp(scores - new_max[..., None]), 0.0)
    rescale = jnp.exp(running_max - new_max)
    products = jnp.einsum(
        "hgqk,khd->hgqd",
        weights.astype(jnp.bfloat16),
        value_head_rows,
        preferred_element_type=jnp.float32,
    )
    summed = summed * rescale[..., None] + products
    totals = totals * rescale + jnp.sum(weights, axis=-1)
    return (new_max, summed, totals)


def fresh_state(kv_heads, group_width, rows_here):
    return (
        jnp.full((kv_heads, group_width, rows_here), -1e30, jnp.float32),
        jnp.zeros((kv_heads, group_width, rows_here, HEAD_SIZE), jnp.float32),
        jnp.zeros((kv_heads, group_width, rows_here), jnp.float32),
    )


def finish(state_now, rows_here, q_heads):
    running_max, summed, totals = state_now
    attended = summed / totals[..., None]
    return (
        jnp.transpose(attended, (2, 0, 1, 3))
        .reshape(rows_here, q_heads * HEAD_SIZE)
        .astype(jnp.bfloat16)
    )


def per_device(queries, keys, values, doc_of_block, out_weight):
    tok_rows = queries.shape[0]
    kv_heads = keys.shape[1] // HEAD_SIZE
    q_heads = queries.shape[1] // HEAD_SIZE
    group_width = q_heads // kv_heads
    ctx_count = lax.axis_size("ctx")
    reach_devs = min(8, ctx_count // 2)
    ctx_index = lax.axis_index("ctx")
    query_start = ctx_index * tok_rows
    query_pos = query_start + jnp.arange(tok_rows, dtype=jnp.int32)
    query_doc = lookup_docs(query_pos, doc_of_block)
    query_head_rows = queries.reshape(tok_rows, kv_heads, group_width, HEAD_SIZE)

    def attend(state_now, key_piece, value_piece, key_start):
        key_pos = key_start + jnp.arange(key_piece.shape[0], dtype=jnp.int32)
        key_doc = lookup_docs(key_pos, doc_of_block)
        visible = (key_doc[None, :] == query_doc[:, None]) & (
            key_pos[None, :] <= query_pos[:, None]
        )
        return update(state_now, query_head_rows, key_piece, value_piece, visible)

    initial_state = fresh_state(kv_heads, group_width, tok_rows)
    state_now = attend(initial_state, keys, values, query_start)
    for distance in range(1, reach_devs + 1):
        prior_keys, prior_values = passed_along((keys, values), "ctx", distance)
        state_now = attend(state_now, prior_keys, prior_values, query_start - distance * tok_rows)
    attended = finish(state_now, tok_rows, q_heads)
    features = lax.all_gather(attended, "head", axis=1, tiled=True)
    mixed = jnp.dot(
        features,
        lax.all_gather(out_weight, "ctx", axis=0, tiled=True),
        preferred_element_type=jnp.float32,
    )
    return mixed.astype(jnp.bfloat16)


def solution(mesh):
    return jax.shard_map(
        per_device,
        mesh=mesh,
        in_specs=(
            P(("group", "ctx"), "head"),
            P(("group", "ctx"), "head"),
            P(("group", "ctx"), "head"),
            P("group"),
            P("ctx", "head"),
        ),
        out_specs=P(("group", "ctx"), "head"),
        check_vma=False,
    )
```

profile of v0, /device:TPU:0, one launch (start us, length us, event | category | flops | bytes accessed | tf_op | source)
XLA Modules:
  0.0 352.3 jit_solution(2587613839477615480)
XLA Ops:
  6.5 1.1 copy.50
  7.6 6.0 %collective-permute-start.6 = (bf16[256,512]{0,1:T(8,128)(2,1)S(1)}, bf16[256,512]{0,1:T(8,128)(2,1)S(1)}, u32[]{:S(2)}, u32[]{:S(2)}) collective-permute-start(bf16[256,512]{0,1:T(8,128)(2,1)S(1)} %copy.50), channel_id=1, source_target_pairs={{0,8},{2,10},{4,12},{6,14},{1,9},{3,11},{5,13},{7,15},{16,24},{18,... | collective-permute-start | bytes 786440 | tf_op jit(solution)/shard_map/ppermute | solution.py:14
  13.6 4.4 %collective-permute-start.4 = (bf16[256,512]{0,1:T(8,128)(2,1)S(1)}, bf16[256,512]{0,1:T(8,128)(2,1)S(1)}, u32[]{:S(2)}, u32[]{:S(2)}) collective-permute-start(bf16[256,512]{0,1:T(8,128)(2,1)S(1)} %copy.50), channel_id=1, source_target_pairs={{0,6},{2,8},{4,10},{6,12},{8,14},{1,7},{3,9},{5,11},{7,13},{9,15},... | collective-permute-start | bytes 786440 | tf_op jit(solution)/shard_map/ppermute | solution.py:14
  18.0 1.3 collective-permute-start.2
  19.4 3.1 collective-permute-start
  22.5 2.7 collective-permute-start.1
  25.2 1.0 reshape.264
  26.2 0.0 copy-start.4
  26.2 1.9 copy.87
  28.2 1.8 reshape.265
  30.0 0.8 select_reduce_fusion
  30.7 0.5 compare_and_fusion.4
  31.3 1.0 fusion
  32.3 0.0 collective-permute-done.6
  32.3 2.6 collective-permute-start.3
  34.9 2.9 fusion.4
  37.8 0.0 collective-permute-done.4
  37.8 2.6 collective-permute-start.5
  40.4 3.0 fusion.3
  43.4 0.0 collective-permute-done.2
  43.4 4.1 %collective-permute-start.7 = (bf16[256,512]{1,0:T(8,128)(2,1)S(1)}, bf16[256,512]{1,0:T(8,128)(2,1)S(1)}, u32[]{:S(2)}, u32[]{:S(2)}) collective-permute-start(bf16[256,512]{1,0:T(8,128)(2,1)S(1)} %copy-done.4), channel_id=1, source_target_pairs={{0,8},{2,10},{4,12},{6,14},{1,9},{3,11},{5,13},{7,15},{16,24},{18,... | collective-permute-start | bytes 786440 | tf_op jit(solution)/shard_map/ppermute | solution.py:14
  47.5 3.0 fusion.2
  50.5 0.0 collective-permute-done
  50.5 1.0 fusion.1
  51.6 1.0 fusion.5
  52.6 2.5 fusion.23
  55.2 1.0 fusion.7
  56.2 0.0 collective-permute-done.1
  56.2 0.1 copy.53
  56.4 4.9 %fusion.21 = f32[4,4,256,128]{2,3,1,0:T(8,128)} fusion(bf16[256,4,128,1]{0,2,3,1:T(8,128)(2,1)S(1)} %bitcast.249, f32[4,256,256,4]{2,1,3,0:T(8,128)} %copy-done.3, f32[4,4,256]{2,1,0:T(4,128)S(1)} %get-tuple-element.17, pred[256,256]{0,1:T(8,128)(4,1)S(1)} %get-tuple-element.22), kind=kOutput, calls=%fused_computation.29 | convolution fusion | flops 273678336 | bytes 6635520 | tf_op jit(solution)/shard_map/hgqk,khd->hgqd/dot_general | solution.py:41
  61.2 1.0 fusion.9
  62.3 0.0 collective-permute-done.3
  62.3 1.1 copy.58
  63.4 4.9 %fusion.19 = f32[4,4,256,128]{2,3,1,0:T(8,128)} fusion(bf16[256,4,128,1]{0,2,3,1:T(8,128)(2,1)S(1)} %bitcast.250, f32[4,256,256,4]{2,1,3,0:T(8,128)} %get-tuple-element.31, f32[4,4,256]{2,1,0:T(4,128)S(1)} %get-tuple-element.16, pred[256,256]{0,1:T(8,128)(4,1)S(1)} %get-tuple-element.24), kind=kOutput, calls=%fused_computation.28 | convolution fusion | flops 273678336 | bytes 6635520 | tf_op jit(solution)/shard_map/hgqk,khd->hgqd/dot_general | solution.py:41
  68.3 1.0 fusion.11
  69.3 0.0 collective-permute-done.5
  69.3 0.1 copy.63
  69.5 4.9 %fusion.17 = f32[4,4,256,128]{2,3,1,0:T(8,128)} fusion(bf16[256,4,128,1]{0,2,3,1:T(8,128)(2,1)S(1)} %bitcast.251, f32[4,256,256,4]{2,1,3,0:T(8,128)} %get-tuple-element.29, f32[4,4,256]{2,1,0:T(4,128)S(1)} %get-tuple-element.15, pred[256,256]{0,1:T(8,128)(4,1)S(1)} %get-tuple-element.23), kind=kOutput, calls=%fused_computation.27 | convolution fusion | flops 273678336 | bytes 6635520 | tf_op jit(solution)/shard_map/hgqk,khd->hgqd/dot_general | solution.py:41
  74.4 1.0 fusion.13
  75.5 0.0 collective-permute-done.7
  75.5 0.4 copy.68
  75.8 7.4 %fusion.26 = bf16[256,4,4,128]{0,3,2,1:T(8,128)(2,1)} fusion(f32[4,4,256,128]{2,3,1,0:T(8,128)} %fusion.17, f32[4,4,256,128]{2,3,1,0:T(8,128)} %fusion.19, f32[4,4,256,128]{2,3,1,0:T(8,128)} %fusion.21, f32[4,4,256,128]{2,3,1,0:T(8,128)} %fusion.23, f32[256,4,4]{0,2,1:T(4,128)S(1)} %get-tuple-element.10, f32[256,4,4]{0,2,1:T(4,128)S(1)} %get-tuple-element.13, ...), kind=kOutput, calls=%fused_computation.33 | convolution fusion | flops 279445504 | bytes 14073856 | tf_op jit(solution)/shard_map/hgqk,khd->hgqd/dot_general | solution.py:41
  83.2 0.0 all-gather.3.cloned.1.call-update
  83.2 0.0 all-gather.5.cloned.1.call-start
  83.3 0.7 all-gather.5.cloned.1.call-update
  84.0 19.0 %all-gather.3.cloned.1.call-done = bf16[256,4096]{0,1:T(8,128)(2,1)} async-done(((bf16[256,2048]{0,1:T(8,128)(2,1)}), bf16[256,4096]{0,1:T(8,128)(2,1)}) %all-gather.3.cloned.1.call-update) | async-done | bytes 2097168 | tf_op jit(solution)/shard_map/all_gather | solution.py:97
  103.0 230.6 %all-gather.5.cloned.1.call-done = bf16[4096,2048]{1,0:T(8,128)(2,1)} async-done(((bf16[512,2048]{1,0:T(8,128)(2,1)}), bf16[4096,2048]{1,0:T(8,128)(2,1)}) %all-gather.5.cloned.1.call-update) | async-done | bytes 16777232 | tf_op jit(solution)/shard_map/all_gather | solution.py:100
  333.6 11.9 %convolution_convert_fusion = bf16[256,2048]{1,0:T(8,128)(2,1)} fusion(bf16[256,4096]{0,1:T(8,128)(2,1)} %all-gather.3.cloned.1.call-done, bf16[4096,2048]{1,0:T(8,128)(2,1)} %all-gather.5.cloned.1.call-done), kind=kOutput, calls=%fused_computation.25 | convolution fusion | flops 4295491584 | bytes 19922944 | tf_op jit(solution)/shard_map/dot_general | solution.py:98
  (19 shorter events, 0.1 us)
Async XLA Ops:
  6.5 96.4 %all-gather.3.cloned.1.call-start = ((), (), s32[]{:S(2)}) async-start(), calls=%async_computation | async-start | bytes 3145728 | tf_op jit(solution)/shard_map/all_gather | solution.py:97
  7.6 24.6 %collective-permute-start.6 = (bf16[256,512]{0,1:T(8,128)(2,1)S(1)}, bf16[256,512]{0,1:T(8,128)(2,1)S(1)}, u32[]{:S(2)}, u32[]{:S(2)}) collective-permute-start(bf16[256,512]{0,1:T(8,128)(2,1)S(1)} %copy.50), channel_id=1, source_target_pairs={{0,8},{2,10},{4,12},{6,14},{1,9},{3,11},{5,13},{7,15},{16,24},{18,... | collective-permute-start | bytes 786440 | tf_op jit(solution)/shard_map/ppermute | solution.py:14
  13.6 24.2 %collective-permute-start.4 = (bf16[256,512]{0,1:T(8,128)(2,1)S(1)}, bf16[256,512]{0,1:T(8,128)(2,1)S(1)}, u32[]{:S(2)}, u32[]{:S(2)}) collective-permute-start(bf16[256,512]{0,1:T(8,128)(2,1)S(1)} %copy.50), channel_id=1, source_target_pairs={{0,6},{2,8},{4,10},{6,12},{8,14},{1,7},{3,9},{5,11},{7,13},{9,15},... | collective-permute-start | bytes 786440 | tf_op jit(solution)/shard_map/ppermute | solution.py:14
  18.0 25.4 %collective-permute-start.2 = (bf16[256,512]{0,1:T(8,128)(2,1)S(1)}, bf16[256,512]{0,1:T(8,128)(2,1)S(1)}, u32[]{:S(2)}, u32[]{:S(2)}) collective-permute-start(bf16[256,512]{0,1:T(8,128)(2,1)S(1)} %copy.50), channel_id=1, source_target_pairs={{0,4},{2,6},{4,8},{6,10},{8,12},{10,14},{1,5},{3,7},{5,9},{7,11},{... | collective-permute-start | bytes 786440 | tf_op jit(solution)/shard_map/ppermute | solution.py:14
  19.4 31.1 %collective-permute-start = (bf16[256,512]{0,1:T(8,128)(2,1)S(1)}, bf16[256,512]{0,1:T(8,128)(2,1)S(1)}, u32[]{:S(2)}, u32[]{:S(2)}) collective-permute-start(bf16[256,512]{0,1:T(8,128)(2,1)S(1)} %copy.50), channel_id=1, source_target_pairs={{0,2},{2,4},{4,6},{6,8},{8,10},{10,12},{12,14},{1,3},{3,5},{5,7},{... | collective-permute-start | bytes 786440 | tf_op jit(solution)/shard_map/ppermute | solution.py:14
  22.5 33.7 %collective-permute-start.1 = (bf16[256,512]{1,0:T(8,128)(2,1)}, bf16[256,512]{1,0:T(8,128)(2,1)S(1)}, u32[]{:S(2)}, u32[]{:S(2)}) collective-permute-start(bf16[256,512]{1,0:T(8,128)(2,1)} %param.7), channel_id=1, source_target_pairs={{0,2},{2,4},{4,6},{6,8},{8,10},{10,12},{12,14},{1,3},{3,5},{5,7},{... | collective-permute-start | bytes 786440 | tf_op jit(solution)/shard_map/ppermute | solution.py:14
  26.2 6.1 %copy-start.4 = (bf16[256,512]{1,0:T(8,128)(2,1)S(1)}, bf16[256,512]{1,0:T(8,128)(2,1)}, u32[]{:S(2)}) copy-start(bf16[256,512]{1,0:T(8,128)(2,1)} %param.7) | copy-start | bytes 786436
  32.3 30.0 %collective-permute-start.3 = (bf16[256,512]{1,0:T(8,128)(2,1)S(1)}, bf16[256,512]{1,0:T(8,128)(2,1)}, u32[]{:S(2)}, u32[]{:S(2)}) collective-permute-start(bf16[256,512]{1,0:T(8,128)(2,1)S(1)} %copy-done.4), channel_id=1, source_target_pairs={{0,4},{2,6},{4,8},{6,10},{8,12},{10,14},{1,5},{3,7},{5,9},{7,11},{... | collective-permute-start | bytes 786440 | tf_op jit(solution)/shard_map/ppermute | solution.py:14
  37.8 31.5 %collective-permute-start.5 = (bf16[256,512]{1,0:T(8,128)(2,1)S(1)}, bf16[256,512]{1,0:T(8,128)(2,1)S(1)}, u32[]{:S(2)}, u32[]{:S(2)}) collective-permute-start(bf16[256,512]{1,0:T(8,128)(2,1)S(1)} %copy-done.4), channel_id=1, source_target_pairs={{0,6},{2,8},{4,10},{6,12},{8,14},{1,7},{3,9},{5,11},{7,13},{9,15},... | collective-permute-start | bytes 786440 | tf_op jit(solution)/shard_map/ppermute | solution.py:14
  43.4 32.0 %collective-permute-start.7 = (bf16[256,512]{1,0:T(8,128)(2,1)S(1)}, bf16[256,512]{1,0:T(8,128)(2,1)S(1)}, u32[]{:S(2)}, u32[]{:S(2)}) collective-permute-start(bf16[256,512]{1,0:T(8,128)(2,1)S(1)} %copy-done.4), channel_id=1, source_target_pairs={{0,8},{2,10},{4,12},{6,14},{1,9},{3,11},{5,13},{7,15},{16,24},{18,... | collective-permute-start | bytes 786440 | tf_op jit(solution)/shard_map/ppermute | solution.py:14
  50.5 2.1 copy-start.5
  51.5 3.6 %copy-start.3 = (f32[4,256,256,4]{2,1,3,0:T(8,128)}, f32[4,256,256,4]{2,1,3,0:T(8,128)S(1)}, u32[]{:S(2)}) copy-start(f32[4,256,256,4]{2,1,3,0:T(8,128)S(1)} %get-tuple-element.33) | copy-start | bytes 12582916
  56.4 4.9 %copy-start.2 = (f32[4,256,256,4]{2,1,3,0:T(8,128)S(1)}, f32[4,256,256,4]{2,1,3,0:T(8,128)}, u32[]{:S(2)}) copy-start(f32[4,256,256,4]{2,1,3,0:T(8,128)} %get-tuple-element.31) | copy-start | bytes 12582916
  63.4 4.9 %copy-start.1 = (f32[4,256,256,4]{2,1,3,0:T(8,128)S(1)}, f32[4,256,256,4]{2,1,3,0:T(8,128)}, u32[]{:S(2)}) copy-start(f32[4,256,256,4]{2,1,3,0:T(8,128)} %get-tuple-element.29) | copy-start | bytes 12582916
  69.5 4.9 %copy-start = (f32[4,256,256,4]{2,1,3,0:T(8,128)S(1)}, f32[4,256,256,4]{2,1,3,0:T(8,128)}, u32[]{:S(2)}) copy-start(f32[4,256,256,4]{2,1,3,0:T(8,128)} %get-tuple-element.27) | copy-start | bytes 12582916
  83.2 250.4 %all-gather.5.cloned.1.call-start = ((), (), s32[]{:S(2)}) async-start(), calls=%async_computation.1 | async-start | bytes 18874368 | tf_op jit(solution)/shard_map/all_gather | solution.py:100
Sparse Core Ops, SparseCore 0:
  83.3 19.5 all-gather.2
  105.1 228.4 all-gather.4
where the time goes:
time: 353 us; the launch traced here: 352 us
  waiting for transfers between devices  250 us (71%)
  matrix products  47.2 us (13%)
  starting transfers between devices  26.9 us (8%)
  between operations  13.7 us (4%)
  local copies, waits for them, and re-layouts  7.47 us (2%)
  other arithmetic  6.66 us (2%)
    all_gather x1, waiting for transfers between devices, per_device(): lax.all_gather(out_weight, 'ctx', axis=0, tiled=True)  231 us
    ppermute x8, starting transfers between devices, passed_along(): return lax.ppermute(array, axis, pairs)  26.9 us
    dot_general x5, matrix products, update(): jnp.einsum('hgqk,khd->hgqd', weights.astype(jnp.bfloat16), value_head_row...  24.5 us
    all_gather x1, waiting for transfers between devices, per_device(): features = lax.all_gather(attended, 'head', axis=1, tiled=True)  19 us
    dot_general x1, matrix products, per_device(): jnp.dot(features, lax.all_gather(out_weight, 'ctx', axis=0, tiled=True),...  11.9 us
    dot_general x5, matrix products, update(): jnp.einsum('qhgd,khd->hgqk', query_head_rows, key_head_rows, preferred_el...  10.8 us
  transfers between devices with their start and end apart: 10, of which 2 were waited for; matrix products, arithmetic and copies ran while one was open for 12% of the time, Pallas kernels for 0%

commit v1 on v0

--- a/solution.py
+++ b/solution.py
@@ -6,6 +6,12 @@
 
 HEAD_SIZE = 128
 BLOCK_TOKENS = 128
+
+
+def guide_pools(xin, which_dim):
+    everything = list(xin.shape[1:])
+    everything[which_dim] *= xin.shape[0]
+    return jnp.moveaxis(xin, 0, which_dim).reshape(everything)
 
 
 def passed_along(array, axis, by):
@@ -95,10 +101,30 @@
         state_now = attend(state_now, prior_keys, prior_values, query_start - distance * tok_rows)
     attended = finish(state_now, tok_rows, q_heads)
     features = lax.all_gather(attended, "head", axis=1, tiled=True)
+
+    def compute_chains_all(dim_no, local_x, mesh_name="ctx"):
+        total_devices = jax.lax.axis_size(mesh_name)
+        windows = tuple(((kk, (kk + 1) % total_devices) for kk in range(total_devices)))
+        u_next, view_out = ([], [])
+        so_far_all = tuple(((num, k) for k, num in windows))
+        for dd in range(total_devices - 1):
+            if dd % 2 == 0:
+                u_next.append(
+                    jax.lax.ppermute(
+                        u_next[-1] if u_next else local_x, axis_name=mesh_name, perm=windows
+                    )
+                )
+            else:
+                view_out.append(
+                    jax.lax.ppermute(view_out[-1] if view_out else local_x, mesh_name, so_far_all)
+                )
+        last = jnp.stack([*u_next[::-1], local_x, *view_out])
+        a_next = jax.lax.axis_index(mesh_name) - len(u_next)
+        last = last[(jnp.arange(total_devices) - a_next) % total_devices]
+        return guide_pools(last, dim_no)
+
     mixed = jnp.dot(
-        features,
-        lax.all_gather(out_weight, "ctx", axis=0, tiled=True),
-        preferred_element_type=jnp.float32,
+        features, compute_chains_all(0, local_x=out_weight), preferred_element_type=jnp.float32
     )
     return mixed.astype(jnp.bfloat16)
 

time: 353 us -> 441 us (1.25); the launches traced: 352 us -> 433 us
  starting transfers between devices: 26.9 us -> 73.6 us
  local copies, waits for them, and re-layouts: 7.47 us -> 44.4 us
  other arithmetic: 6.66 us -> 21.1 us
  matrix products: 47.2 us -> 34.8 us
  waiting for transfers between devices: 250 us -> 245 us
    all_gather x1 -> x0, waiting for transfers between devices: 231 us -> none  [per_device(): lax.all_gather(out_weight, 'ctx', axis=0, tiled=True)]
    ppermute x0 -> x7, waiting for transfers between devices: none -> 219 us  [the longest x3 110 us: compute_chains_all(): jax.lax.ppermute(view_out[-1] if view_out else local_x, mesh_name, so_far...]
    ppermute x8, starting transfers between devices: 26.9 us -> 55.7 us  [passed_along(): return lax.ppermute(array, axis, pairs)]
    ppermute x8, waiting for transfers between devices: 0.02 us -> 26.1 us  [passed_along(): return lax.ppermute(array, axis, pairs)]
    gather x0 -> x3, local copies, waits for them, and re-layouts: none -> 22.6 us  [compute_chains_all(): last = last[(jnp.arange(total_devices) - a_next) % total_devices]]
    all_gather x1, waiting for transfers between devices: 19 us -> 0.01 us  [per_device(): features = lax.all_gather(attended, 'head', axis=1, tiled=True)]
    ppermute x0 -> x7, starting transfers between devices: none -> 17.9 us  [the longest x4 10.3 us: compute_chains_all(): jax.lax.ppermute(u_next[-1] if u_next else local_x, axis_name=mesh_name,...]
    unnamed x0 -> x1, other arithmetic: none -> 13.8 us
  transfers between devices with their start and end apart: 10 -> 16, of which waited for: 2 -> 5; matrix products, arithmetic and copies ran while one was open for 12% -> 20% of each run, Pallas kernels for 0% -> 0%
where the time goes in v1:
time: 441 us; the launch traced here: 433 us
  waiting for transfers between devices  245 us (56%)
  starting transfers between devices  73.6 us (17%)
  local copies, waits for them, and re-layouts  44.4 us (10%)
  matrix products  34.8 us (8%)
  other arithmetic  21.1 us (5%)
  between operations  13.8 us (3%)
    ppermute x3, waiting for transfers between devices, compute_chains_all(): jax.lax.ppermute(view_out[-1] if view_out else local_x, mesh_name, so_far...  110 us
    ppermute x4, waiting for transfers between devices, compute_chains_all(): jax.lax.ppermute(u_next[-1] if u_next else local_x, axis_name=mesh_name,...  109 us
    ppermute x8, starting transfers between devices, passed_along(): return lax.ppermute(array, axis, pairs)  55.7 us
    ppermute x8, waiting for transfers between devices, passed_along(): return lax.ppermute(array, axis, pairs)  26.1 us
    gather x3, local copies, waits for them, and re-layouts, compute_chains_all(): last = last[(jnp.arange(total_devices) - a_next) % total_devices]  22.6 us
    unnamed x1, other arithmetic  13.8 us
    unnamed x36, local copies, waits for them, and re-layouts  13 us
    dot_general x5, matrix products, update(): jnp.einsum('hgqk,khd->hgqd', weights.astype(jnp.bfloat16), value_head_row...  12.8 us
  transfers between devices with their start and end apart: 16, of which 5 were waited for; matrix products, arithmetic and copies ran while one was open for 20% of the time, Pallas kernels for 0%

profile of v1, /device:TPU:0, one launch (start us, length us, event | category | flops | bytes accessed | tf_op | source)
XLA Modules:
  0.0 432.6 jit_solution(17743669794512715866)
XLA Ops:
  6.5 3.0 collective-permute-start.8
  9.5 1.8 copy.50
  11.3 4.5 %collective-permute-start.6 = (bf16[256,512]{0,1:T(8,128)(2,1)}, bf16[256,512]{0,1:T(8,128)(2,1)S(1)}, u32[]{:S(2)}, u32[]{:S(2)}) collective-permute-start(bf16[256,512]{0,1:T(8,128)(2,1)} %copy.50), channel_id=1, source_target_pairs={{0,8},{2,10},{4,12},{6,14},{1,9},{3,11},{5,13},{7,15},{16,24},{18,... | collective-permute-start | bytes 786440 | tf_op jit(solution)/shard_map/ppermute | solution.py:20
  15.8 2.9 collective-permute-start.4
  18.7 2.6 collective-permute-start.2
  21.3 3.3 collective-permute-start.1
  25.7 1.8 copy.87
  27.5 1.8 reshape.317
  31.3 2.9 fusion
  34.2 26.1 %collective-permute-done.1 = bf16[256,512]{1,0:T(8,128)(2,1)S(1)} collective-permute-done((bf16[256,512]{1,0:T(8,128)(2,1)}, bf16[256,512]{1,0:T(8,128)(2,1)S(1)}, u32[]{:S(2)}, u32[]{:S(2)}) %collective-permute-start.1) | collective-permute-done | bytes 262176 | tf_op jit(solution)/shard_map/ppermute | solution.py:20
  60.3 21.1 %collective-permute-start = (bf16[256,512]{0,1:T(8,128)(2,1)}, bf16[256,512]{0,1:T(8,128)(2,1)}, u32[]{:S(2)}, u32[]{:S(2)}) collective-permute-start(bf16[256,512]{0,1:T(8,128)(2,1)} %copy.50), channel_id=1, source_target_pairs={{0,2},{2,4},{4,6},{6,8},{8,10},{10,12},{12,14},{1,3},{3,5},{5,7},{... | collective-permute-start | bytes 786440 | tf_op jit(solution)/shard_map/ppermute | solution.py:20
  82.3 14.7 %collective-permute-start.3 = (bf16[256,512]{1,0:T(8,128)(2,1)}, bf16[256,512]{1,0:T(8,128)(2,1)}, u32[]{:S(2)}, u32[]{:S(2)}) collective-permute-start(bf16[256,512]{1,0:T(8,128)(2,1)} %param.7), channel_id=1, source_target_pairs={{0,4},{2,6},{4,8},{6,10},{8,12},{10,14},{1,5},{3,7},{5,9},{7,11},{... | collective-permute-start | bytes 786440 | tf_op jit(solution)/shard_map/ppermute | solution.py:20
  97.0 3.3 collective-permute-start.9
  101.3 2.0 collective-permute-start.5
  103.4 2.1 fusion.3
  105.5 4.5 %collective-permute-start.7 = (bf16[256,512]{1,0:T(8,128)(2,1)}, bf16[256,512]{1,0:T(8,128)(2,1)}, u32[]{:S(2)}, u32[]{:S(2)}) collective-permute-start(bf16[256,512]{1,0:T(8,128)(2,1)} %param.7), channel_id=1, source_target_pairs={{0,8},{2,10},{4,12},{6,14},{1,9},{3,11},{5,13},{7,15},{16,24},{18,... | collective-permute-start | bytes 786440 | tf_op jit(solution)/shard_map/ppermute | solution.py:20
  110.0 2.0 fusion.2
  112.1 2.2 fusion.1
  114.3 1.0 fusion.11
  115.4 73.6 %collective-permute-done.9 = bf16[512,2048]{1,0:T(8,128)(2,1)S(1)} collective-permute-done((bf16[512,2048]{1,0:T(8,128)(2,1)}, bf16[512,2048]{1,0:T(8,128)(2,1)S(1)}, u32[]{:S(2)}, u32[]{:S(2)}) %collective-permute-start.9) | collective-permute-done | bytes 2097184 | tf_op jit(solution)/shard_map/ppermute | solution.py:113
  189.0 2.4 collective-permute-start.10
  191.4 1.0 fusion.13
  192.4 1.0 fusion.7
  193.5 1.0 fusion.5
  194.6 2.5 fusion.23
  197.2 2.5 fusion.21
  199.7 2.3 collective-permute-start.13
  202.1 34.9 %collective-permute-done.10 = bf16[512,2048]{1,0:T(8,128)(2,1)} collective-permute-done((bf16[512,2048]{1,0:T(8,128)(2,1)S(1)}, bf16[512,2048]{1,0:T(8,128)(2,1)}, u32[]{:S(2)}, u32[]{:S(2)}) %collective-permute-start.10) | collective-permute-done | bytes 2097184 | tf_op jit(solution)/shard_map/ppermute | solution.py:113
  237.0 1.7 collective-permute-start.11
  239.7 1.1 copy.58
  240.8 1.1 copy.63
  241.9 1.1 copy.68
  243.1 3.5 fusion.19
  246.6 1.2 fusion.17
  249.5 2.9 fusion.26
  252.5 74.3 %collective-permute-done.13 = bf16[512,2048]{1,0:T(8,128)(2,1)} collective-permute-done((bf16[512,2048]{1,0:T(8,128)(2,1)}, bf16[512,2048]{1,0:T(8,128)(2,1)}, u32[]{:S(2)}, u32[]{:S(2)}) %collective-permute-start.13) | collective-permute-done | bytes 2097184 | tf_op jit(solution)/shard_map/ppermute | solution.py:119
  326.8 5.2 %collective-permute-start.14 = (bf16[512,2048]{1,0:T(8,128)(2,1)}, bf16[512,2048]{1,0:T(8,128)(2,1)S(1)}, u32[]{:S(2)}, u32[]{:S(2)}) collective-permute-start(bf16[512,2048]{1,0:T(8,128)(2,1)} %collective-permute-done.13), channel_id=1, source_target_pairs={{2,0},{4,2},{6,4},{8,6},{10,8},{12,10},{14,12},{0,14},{3,1},{5,3},... | collective-permute-start | bytes 6291464 | tf_op jit(solution)/shard_map/ppermute | solution.py:119
  332.0 1.8 bitcast_dynamic-update-slice_fusion.7
  333.8 1.8 bitcast_dynamic-update-slice_fusion.6
  335.8 1.8 bitcast_dynamic-update-slice_fusion.4
  337.8 1.8 bitcast_dynamic-update-slice_fusion.2
  339.6 1.8 bitcast_dynamic-update-slice_fusion.1
  341.5 35.9 %collective-permute-done.14 = bf16[512,2048]{1,0:T(8,128)(2,1)S(1)} collective-permute-done((bf16[512,2048]{1,0:T(8,128)(2,1)}, bf16[512,2048]{1,0:T(8,128)(2,1)S(1)}, u32[]{:S(2)}, u32[]{:S(2)}) %collective-permute-start.14) | collective-permute-done | bytes 2097184 | tf_op jit(solution)/shard_map/ppermute | solution.py:119
  377.5 6.2 %fusion.98 = (bf16[8,512,1024]{2,1,0:T(8,128)(2,1)}, bf16[8,512,1024]{2,1,0:T(8,128)(2,1)}) fusion(bf16[8,512,2048]{2,1,0:T(8,128)(2,1)S(1)} %bitcast_dynamic-update-slice_fusion), kind=kLoop, calls=%fused_computation.175 | loop fusion | bytes 33554432 | tf_op jit(solution)/shard_map/gather | solution.py:123
  383.7 8.2 %gather_fusion = bf16[8,512,1024]{2,1,0:T(8,128)(2,1)} fusion(bf16[8,512,1024]{2,1,0:T(8,128)(2,1)} %get-tuple-element.18, s32[1024]{0:T(1024)} %pad_clamp_fusion), kind=kCustom, calls=%fused_computation | custom fusion | bytes 16777248 | tf_op jit(solution)/shard_map/gather | solution.py:123
  391.9 8.2 %gather_fusion.1 = bf16[8,512,1024]{2,1,0:T(8,128)(2,1)} fusion(bf16[8,512,1024]{2,1,0:T(8,128)(2,1)} %get-tuple-element.19, s32[1024]{0:T(1024)} %pad_clamp_fusion), kind=kCustom, calls=%fused_computation.1 | custom fusion | bytes 16777248 | tf_op jit(solution)/shard_map/gather | solution.py:123
  400.1 13.8 %pad_maximum_fusion = bf16[8,512,2048]{2,1,0:T(8,128)(2,1)} fusion(bf16[8,512,1024]{2,1,0:T(8,128)(2,1)} %gather_fusion.1, bf16[8,512,1024]{2,1,0:T(8,128)(2,1)} %gather_fusion), kind=kLoop, calls=%fused_computation.2 | loop fusion | flops 33554432 | bytes 33554432
  413.9 11.9 %convolution_convert_fusion = bf16[256,2048]{1,0:T(8,128)(2,1)} fusion(bf16[256,4096]{0,1:T(8,128)(2,1)} %all-gather.2.cloned.1.call-done, bf16[4096,2048]{1,0:T(8,128)(2,1)} %bitcast.260), kind=kOutput, calls=%fused_computation.28 | convolution fusion | flops 4295491584 | bytes 19922944 | tf_op jit(solution)/shard_map/dot_general | solution.py:126
  (60 shorter events, 8.3 us)
Async XLA Ops:
  6.5 407.4 %all-gather.2.cloned.1.call-start = ((), (), s32[]{:S(2)}) async-start(), calls=%async_computation | async-start | bytes 3145728 | tf_op jit(solution)/shard_map/all_gather | solution.py:103
  6.5 90.4 %collective-permute-start.8 = (bf16[512,2048]{1,0:T(8,128)(2,1)}, bf16[512,2048]{1,0:T(8,128)(2,1)}, u32[]{:S(2)}, u32[]{:S(2)}) collective-permute-start(bf16[512,2048]{1,0:T(8,128)(2,1)} %param.9), channel_id=1, source_target_pairs={{0,2},{2,4},{4,6},{6,8},{8,10},{10,12},{12,14},{14,0},{1,3},{3,5},... | collective-permute-start | bytes 6291464 | tf_op jit(solution)/shard_map/ppermute | solution.py:113
  11.3 71.0 %collective-permute-start.6 = (bf16[256,512]{0,1:T(8,128)(2,1)}, bf16[256,512]{0,1:T(8,128)(2,1)S(1)}, u32[]{:S(2)}, u32[]{:S(2)}) collective-permute-start(bf16[256,512]{0,1:T(8,128)(2,1)} %copy.50), channel_id=1, source_target_pairs={{0,8},{2,10},{4,12},{6,14},{1,9},{3,11},{5,13},{7,15},{16,24},{18,... | collective-permute-start | bytes 786440 | tf_op jit(solution)/shard_map/ppermute | solution.py:20
  15.8 85.5 %collective-permute-start.4 = (bf16[256,512]{0,1:T(8,128)(2,1)}, bf16[256,512]{0,1:T(8,128)(2,1)S(1)}, u32[]{:S(2)}, u32[]{:S(2)}) collective-permute-start(bf16[256,512]{0,1:T(8,128)(2,1)} %copy.50), channel_id=1, source_target_pairs={{0,6},{2,8},{4,10},{6,12},{8,14},{1,7},{3,9},{5,11},{7,13},{9,15},... | collective-permute-start | bytes 786440 | tf_op jit(solution)/shard_map/ppermute | solution.py:20
  18.7 86.8 %collective-permute-start.2 = (bf16[256,512]{0,1:T(8,128)(2,1)}, bf16[256,512]{0,1:T(8,128)(2,1)}, u32[]{:S(2)}, u32[]{:S(2)}) collective-permute-start(bf16[256,512]{0,1:T(8,128)(2,1)} %copy.50), channel_id=1, source_target_pairs={{0,4},{2,6},{4,8},{6,10},{8,12},{10,14},{1,5},{3,7},{5,9},{7,11},{... | collective-permute-start | bytes 786440 | tf_op jit(solution)/shard_map/ppermute | solution.py:20
  21.3 39.0 %collective-permute-start.1 = (bf16[256,512]{1,0:T(8,128)(2,1)}, bf16[256,512]{1,0:T(8,128)(2,1)S(1)}, u32[]{:S(2)}, u32[]{:S(2)}) collective-permute-start(bf16[256,512]{1,0:T(8,128)(2,1)} %param.7), channel_id=1, source_target_pairs={{0,2},{2,4},{4,6},{6,8},{8,10},{10,12},{12,14},{1,3},{3,5},{5,7},{... | collective-permute-start | bytes 786440 | tf_op jit(solution)/shard_map/ppermute | solution.py:20
  60.3 51.7 %collective-permute-start = (bf16[256,512]{0,1:T(8,128)(2,1)}, bf16[256,512]{0,1:T(8,128)(2,1)}, u32[]{:S(2)}, u32[]{:S(2)}) collective-permute-start(bf16[256,512]{0,1:T(8,128)(2,1)} %copy.50), channel_id=1, source_target_pairs={{0,2},{2,4},{4,6},{6,8},{8,10},{10,12},{12,14},{1,3},{3,5},{5,7},{... | collective-permute-start | bytes 786440 | tf_op jit(solution)/shard_map/ppermute | solution.py:20
  82.3 157.4 %collective-permute-start.3 = (bf16[256,512]{1,0:T(8,128)(2,1)}, bf16[256,512]{1,0:T(8,128)(2,1)}, u32[]{:S(2)}, u32[]{:S(2)}) collective-permute-start(bf16[256,512]{1,0:T(8,128)(2,1)} %param.7), channel_id=1, source_target_pairs={{0,4},{2,6},{4,8},{6,10},{8,12},{10,14},{1,5},{3,7},{5,9},{7,11},{... | collective-permute-start | bytes 786440 | tf_op jit(solution)/shard_map/ppermute | solution.py:20
  97.0 92.0 %collective-permute-start.9 = (bf16[512,2048]{1,0:T(8,128)(2,1)}, bf16[512,2048]{1,0:T(8,128)(2,1)S(1)}, u32[]{:S(2)}, u32[]{:S(2)}) collective-permute-start(bf16[512,2048]{1,0:T(8,128)(2,1)} %collective-permute-done.8), channel_id=1, source_target_pairs={{0,2},{2,4},{4,6},{6,8},{8,10},{10,12},{12,14},{14,0},{1,3},{3,5},... | collective-permute-start | bytes 6291464 | tf_op jit(solution)/shard_map/ppermute | solution.py:113
  101.3 90.1 %copy-start = (f32[4,256,256,4]{2,1,3,0:T(8,128)}, f32[4,256,256,4]{2,1,3,0:T(8,128)S(1)}, u32[]{:S(2)}) copy-start(f32[4,256,256,4]{2,1,3,0:T(8,128)S(1)} %get-tuple-element.29) | copy-start | bytes 12582916
  101.3 2.1 copy-start.9
  101.3 139.5 %collective-permute-start.5 = (bf16[256,512]{1,0:T(8,128)(2,1)}, bf16[256,512]{1,0:T(8,128)(2,1)}, u32[]{:S(2)}, u32[]{:S(2)}) collective-permute-start(bf16[256,512]{1,0:T(8,128)(2,1)} %param.7), channel_id=1, source_target_pairs={{0,6},{2,8},{4,10},{6,12},{8,14},{1,7},{3,9},{5,11},{7,13},{9,15},... | collective-permute-start | bytes 786440 | tf_op jit(solution)/shard_map/ppermute | solution.py:20
  103.4 8.7 %copy-start.6 = (bf16[512,2048]{1,0:T(8,128)(2,1)S(1)}, bf16[512,2048]{1,0:T(8,128)(2,1)}, u32[]{:S(2)}) copy-start(bf16[512,2048]{1,0:T(8,128)(2,1)} %param.9) | copy-start | bytes 6291460
  105.5 8.8 %copy-start.2 = (f32[4,256,256,4]{2,1,3,0:T(8,128)}, f32[4,256,256,4]{2,1,3,0:T(8,128)S(1)}, u32[]{:S(2)}) copy-start(f32[4,256,256,4]{2,1,3,0:T(8,128)S(1)} %get-tuple-element.31) | copy-start | bytes 12582916
  105.5 136.4 %collective-permute-start.7 = (bf16[256,512]{1,0:T(8,128)(2,1)}, bf16[256,512]{1,0:T(8,128)(2,1)}, u32[]{:S(2)}, u32[]{:S(2)}) collective-permute-start(bf16[256,512]{1,0:T(8,128)(2,1)} %param.7), channel_id=1, source_target_pairs={{0,8},{2,10},{4,12},{6,14},{1,9},{3,11},{5,13},{7,15},{16,24},{18,... | collective-permute-start | bytes 786440 | tf_op jit(solution)/shard_map/ppermute | solution.py:20
  112.0 126.6 %copy-start.4 = (f32[4,256,256,4]{2,1,3,0:T(8,128)}, f32[4,256,256,4]{2,1,3,0:T(8,128)S(1)}, u32[]{:S(2)}) copy-start(f32[4,256,256,4]{2,1,3,0:T(8,128)S(1)} %get-tuple-element.33) | copy-start | bytes 12582916
  112.0 87.7 %collective-permute-start.12 = (bf16[512,2048]{1,0:T(8,128)(2,1)S(1)}, bf16[512,2048]{1,0:T(8,128)(2,1)}, u32[]{:S(2)}, u32[]{:S(2)}) collective-permute-start(bf16[512,2048]{1,0:T(8,128)(2,1)S(1)} %copy-done.6), channel_id=1, source_target_pairs={{2,0},{4,2},{6,4},{8,6},{10,8},{12,10},{14,12},{0,14},{3,1},{5,3},... | collective-permute-start | bytes 6291464 | tf_op jit(solution)/shard_map/ppermute | solution.py:119
  189.0 4.5 %copy-start.7 = (bf16[512,2048]{1,0:T(8,128)(2,1)}, bf16[512,2048]{1,0:T(8,128)(2,1)S(1)}, u32[]{:S(2)}) copy-start(bf16[512,2048]{1,0:T(8,128)(2,1)S(1)} %collective-permute-done.9) | copy-start | bytes 6291460
  189.0 48.0 %collective-permute-start.10 = (bf16[512,2048]{1,0:T(8,128)(2,1)S(1)}, bf16[512,2048]{1,0:T(8,128)(2,1)}, u32[]{:S(2)}, u32[]{:S(2)}) collective-permute-start(bf16[512,2048]{1,0:T(8,128)(2,1)S(1)} %collective-permute-done.9), channel_id=1, source_target_pairs={{0,2},{2,4},{4,6},{6,8},{8,10},{10,12},{12,14},{14,0},{1,3},{3,5},... | collective-permute-start | bytes 6291464 | tf_op jit(solution)/shard_map/ppermute | solution.py:113
  191.4 2.2 copy-start.5
  192.4 2.2 copy-start.10
  194.6 2.6 copy-start.11
  199.7 127.0 %collective-permute-start.13 = (bf16[512,2048]{1,0:T(8,128)(2,1)}, bf16[512,2048]{1,0:T(8,128)(2,1)}, u32[]{:S(2)}, u32[]{:S(2)}) collective-permute-start(bf16[512,2048]{1,0:T(8,128)(2,1)} %collective-permute-done.12), channel_id=1, source_target_pairs={{2,0},{4,2},{6,4},{8,6},{10,8},{12,10},{14,12},{0,14},{3,1},{5,3},... | collective-permute-start | bytes 6291464 | tf_op jit(solution)/shard_map/ppermute | solution.py:119
  237.0 95.0 %collective-permute-start.11 = (bf16[512,2048]{1,0:T(8,128)(2,1)}, bf16[512,2048]{1,0:T(8,128)(2,1)}, u32[]{:S(2)}, u32[]{:S(2)}) collective-permute-start(bf16[512,2048]{1,0:T(8,128)(2,1)} %collective-permute-done.10), channel_id=1, source_target_pairs={{0,2},{2,4},{4,6},{6,8},{8,10},{10,12},{12,14},{14,0},{1,3},{3,5},... | collective-permute-start | bytes 6291464 | tf_op jit(solution)/shard_map/ppermute | solution.py:113
  243.0 3.6 copy-start.3
  243.1 4.8 %copy-start.13 = (f32[4,4,256,128]{2,3,1,0:T(8,128)S(1)}, f32[4,4,256,128]{2,3,1,0:T(8,128)}, u32[]{:S(2)}) copy-start(f32[4,4,256,128]{2,3,1,0:T(8,128)} %fusion.21) | copy-start | bytes 6291460
  246.6 2.3 copy-start.1
  246.6 2.9 copy-start.12
  252.5 83.2 %copy-start.8 = (bf16[512,2048]{1,0:T(8,128)(2,1)S(1)}, bf16[512,2048]{1,0:T(8,128)(2,1)}, u32[]{:S(2)}) copy-start(bf16[512,2048]{1,0:T(8,128)(2,1)} %copy-done.7) | copy-start | bytes 6291460
  326.8 50.6 %collective-permute-start.14 = (bf16[512,2048]{1,0:T(8,128)(2,1)}, bf16[512,2048]{1,0:T(8,128)(2,1)S(1)}, u32[]{:S(2)}, u32[]{:S(2)}) collective-permute-start(bf16[512,2048]{1,0:T(8,128)(2,1)} %collective-permute-done.13), channel_id=1, source_target_pairs={{2,0},{4,2},{6,4},{8,6},{10,8},{12,10},{14,12},{0,14},{3,1},{5,3},... | collective-permute-start | bytes 6291464 | tf_op jit(solution)/shard_map/ppermute | solution.py:119
Sparse Core Ops, SparseCore 0:
  252.6 44.7 all-gather.1
